TPU v7x, 128 devices: a whole 4x4x4 slice. The times are simulated.
128 devices in a mesh: grp: 4 (over y), tile: 32 (over x, z, core).
Axes of the slice: x: 4, y: 4, z: 4, core: 2. Of those that a mesh axis runs over, the one named last changes fastest.
Arguments:
- amp_tiles: bfloat16 [65536, 64, 64], P(('grp', 'tile')), may hold values from -6 to 6
- amp_row: int32 [65536], P(('grp', 'tile')), may hold values from 0 to 1024, as said below
- amp_col: int32 [65536], P(('grp', 'tile')), may hold values from 0 to 61
- cycle_panel: bfloat16 [3968, 3968], P('grp'), may hold values from -0.09375 to 0.09375
Outputs:
- residual: bfloat16 [65536, 64, 64], P(('grp', 'tile'))
Inputs may be any that keep to these rules, and one draw needn't show every extreme that they name: `amp_row`: tiles n of block k = n // 512 lie in group h = k // 32: their rows are h * 256 to (h + 1) * 256 - 1, or 1024 for an empty slot. No two non-empty tiles name the same row and column tile. Within one block of 512 tiles at most 16 name rows of one run r * 8 to (r + 1) * 8 - 1, and 16 is reached in every draw; in every group some run has all its 496 tiles present.
All inputs are finite; a program needn't handle non-finite values.
Results may differ from a plain program's by a relative error of at most 0.001.
Values may be sent and summed in bfloat16 or wider, within the bound.
No kernel may reach another device: no remote copies, remote signals or barrier semaphores. Data moves between devices by JAX's collectives and lax.ppermute only.
A program may use at most 192 MiB of HBM per device.

v0:
```python
import jax
import jax.numpy as jnp
from jax import lax
from jax.sharding import PartitionSpec as P

ROWT_DEV = 8


def body(amp_tiles, amp_row, amp_col, cycle_panel):
    parts = lax.axis_size("tile")
    count = amp_tiles.shape[0]
    capacity = count // parts
    edge = amp_tiles.shape[1]
    width = cycle_panel.shape[1]
    nvt = width // edge
    per_dest = ROWT_DEV * nvt
    group_rows = ROWT_DEV * parts
    first = lax.axis_index("grp") * group_rows
    local_row = amp_row - first
    live = local_row < group_rows
    target = jnp.where(live, local_row // ROWT_DEV, parts)
    onehot = (target[:, None] == jnp.arange(parts)[None, :]).astype(jnp.int32)
    rank = jnp.sum(jnp.cumsum(onehot, axis=0) * onehot, axis=1) - 1
    position = jnp.where(live, target * capacity + rank, parts * capacity)
    block_id = local_row % ROWT_DEV * nvt + amp_col
    flat = amp_tiles.reshape(count, edge * edge)
    send_tiles = (
        jnp.zeros((parts * capacity, edge * edge), jnp.bfloat16).at[position].set(flat, mode="drop")
    )
    send_ids = (
        jnp.full((parts * capacity,), per_dest, jnp.int32).at[position].set(block_id, mode="drop")
    )
    recv_tiles, recv_ids = (
        lax.all_to_all(send_tiles, "tile", split_axis=0, concat_axis=0, tiled=True),
        lax.all_to_all(send_ids, "tile", split_axis=0, concat_axis=0, tiled=True),
    )
    dense = (
        jnp.zeros((per_dest, edge * edge), jnp.bfloat16).at[recv_ids].set(recv_tiles, mode="drop")
    )
    dense = (
        dense.reshape(ROWT_DEV, nvt, edge, edge)
        .transpose(0, 2, 1, 3)
        .reshape(ROWT_DEV * edge, width)
    )
    cycle = jnp.dot(
        dense,
        lax.all_gather(cycle_panel, "grp", axis=0, tiled=True),
        preferred_element_type=jnp.float32,
    )
    cycle = cycle.astype(jnp.bfloat16)
    blocks_out = (
        cycle.reshape(ROWT_DEV, edge, nvt, edge)
        .transpose(0, 2, 1, 3)
        .reshape(per_dest, edge * edge)
    )
    answer = jnp.take(blocks_out, recv_ids, axis=0, mode="fill", fill_value=0)
    returned = lax.all_to_all(answer, "tile", split_axis=0, concat_axis=0, tiled=True)
    result = jnp.take(returned, position, axis=0, mode="fill", fill_value=0)
    return result.reshape(count, edge, edge)


def solution(mesh):
    in_specs = (
        P(("grp", "tile"), None, None),
        P(("grp", "tile")),
        P(("grp", "tile")),
        P("grp", None),
    )
    out_specs = P(("grp", "tile"), None, None)
    return jax.shard_map(body, mesh=mesh, in_specs=in_specs, out_specs=out_specs, check_vma=False)
```

profile of v0, /device:TPU:1, one launch (start us, length us, event | category | flops | bytes accessed | tf_op | source)
XLA Modules:
  0.0 457.8 jit_solution(15762808413656921646)
XLA Ops:
  6.5 0.0 copy-start
  6.5 0.0 copy-start.1
  6.5 0.0 all-gather.2.cloned.1.call-start
  6.5 0.7 all-gather.2.cloned.1.call-update
  7.3 0.0 copy-done
  7.3 0.0 copy-done.1
  7.3 1.2 reduce-window.6
  8.5 0.2 slice_reduce_fusion
  8.8 0.1 fusion.5
  8.9 2.4 scatter_custom_fusion
  11.3 0.7 all_to_all.24
  12.0 9.4 %all-to-all-start = ((s32[32,16,1]{1,2,0:T(1,128)}), s32[32,16,1]{1,2,0:T(1,128)S(1)}, u32[]{:S(2)}, u32[]{:S(2)}) async-start(s32[32,16,1]{1,2,0:T(1,128)} %bitcast.2), calls=%async_computation | async-start | bytes 32768 | tf_op jit(solution)/shard_map/all_to_all | solution.py:35
  21.4 6.9 %copy.20 = bf16[512,4096]{1,0:T(8,128)(2,1)} copy(bf16[512,4096]{0,1:T(8,128)(2,1)} %bitcast.43) | data formatting | bytes 8388608 | tf_op jit(solution)/shard_map/reshape | solution.py:26
  28.4 10.9 %scatter_custom_fusion.1 = bf16[512,4096]{1,0:T(8,128)(2,1)} fusion(s32[512]{0:T(512)S(1)} %get-tuple-element.6, bf16[512,4096]{1,0:T(8,128)(2,1)} %copy.20, bf16[]{:T(256)} %constant.84.clone.1), kind=kCustom, calls=%fused_computation.8 | custom fusion | bytes 4194816 | tf_op jit(solution)/shard_map/scatter | solution.py:28
  39.3 0.0 all-to-all-done
  39.3 7.5 %all-to-all-start.1 = ((bf16[32,16,4096]{2,1,0:T(8,128)(2,1)}), bf16[32,16,4096]{2,1,0:T(8,128)(2,1)}, u32[]{:S(2)}, u32[]{:S(2)}) async-start(bf16[32,16,4096]{2,1,0:T(8,128)(2,1)} %bitcast.41), calls=%async_computation.1 | async-start | bytes 8388608 | tf_op jit(solution)/shard_map/all_to_all | solution.py:34
  46.8 0.5 broadcast.122
  47.3 0.7 reduce.5
  48.0 0.1 all_to_all.27
  48.1 50.8 %all-to-all-done.1 = bf16[32,16,4096]{2,1,0:T(8,128)(2,1)} async-done(((bf16[32,16,4096]{2,1,0:T(8,128)(2,1)}), bf16[32,16,4096]{2,1,0:T(8,128)(2,1)}, u32[]{:S(2)}, u32[]{:S(2)}) %all-to-all-start.1) | async-done | bytes 4194336 | tf_op jit(solution)/shard_map/all_to_all | solution.py:34
  98.9 10.3 %scatter_custom_fusion.2 = bf16[496,4096]{1,0:T(8,128)(2,1)} fusion(s32[512]{0:T(512)S(1)} %bitcast.47, bf16[512,4096]{1,0:T(8,128)(2,1)} %bitcast.7, bf16[]{:T(256)} %constant.84.clone.1), kind=kCustom, calls=%fused_computation.10 | custom fusion | bytes 4063744 | tf_op jit(solution)/shard_map/scatter | solution.py:38
  109.2 12.1 %reshape.91 = bf16[8,62,64,64]{3,2,1,0:T(8,128)(2,1)} reshape(bf16[496,4096]{1,0:T(8,128)(2,1)} %scatter_custom_fusion.2) | data formatting | bytes 8126464 | tf_op jit(solution)/shard_map/reshape | solution.py:41
  121.3 12.2 %copy.21 = bf16[8,64,62,64]{1,0,3,2:T(8,128)(2,1)} copy(bf16[8,64,62,64]{3,1,2,0:T(8,128)(2,1)} %bitcast.38) | data formatting | bytes 8126464 | tf_op jit(solution)/shard_map/transpose | solution.py:42
  133.5 11.5 %reshape.92 = bf16[512,3968]{0,1:T(8,128)(2,1)} reshape(bf16[8,64,62,64]{1,0,3,2:T(8,128)(2,1)} %copy.21) | data formatting | bytes 8126464 | tf_op jit(solution)/shard_map/reshape | solution.py:43
  145.0 143.5 %all-gather.2.cloned.1.call-done = bf16[3968,3968]{1,0:T(8,128)(2,1)} async-done(((bf16[992,3968]{1,0:T(8,128)(2,1)}), bf16[3968,3968]{1,0:T(8,128)(2,1)}) %all-gather.2.cloned.1.call-update) | async-done | bytes 31490064 | tf_op jit(solution)/shard_map/all_gather | solution.py:47
  288.4 23.6 %convolution_convert_fusion = bf16[512,3968]{1,0:T(8,128)(2,1)} fusion(bf16[512,3968]{0,1:T(8,128)(2,1)} %reshape.92, bf16[3968,3968]{1,0:T(8,128)(2,1)} %all-gather.2.cloned.1.call-done), kind=kOutput, calls=%fused_computation.5 | convolution fusion | flops 16124936192 | bytes 39616512 | tf_op jit(solution)/shard_map/dot_general | solution.py:45
  312.0 6.4 %copy.22 = bf16[512,3968]{0,1:T(8,128)(2,1)} copy(bf16[512,3968]{1,0:T(8,128)(2,1)} %convolution_convert_fusion) | data formatting | bytes 8126464 | tf_op jit(solution)/shard_map/convert_element_type | solution.py:50
  318.3 10.9 %reshape.93 = bf16[8,64,62,64]{1,0,3,2:T(8,128)(2,1)} reshape(bf16[512,3968]{0,1:T(8,128)(2,1)} %copy.22) | data formatting | bytes 8126464 | tf_op jit(solution)/shard_map/reshape | solution.py:52
  329.3 11.7 %copy.23 = bf16[8,62,64,64]{3,2,1,0:T(8,128)(2,1)} copy(bf16[8,62,64,64]{2,0,3,1:T(8,128)(2,1)} %bitcast.39) | data formatting | bytes 8126464 | tf_op jit(solution)/shard_map/transpose | solution.py:53
  341.0 11.7 %reshape.94 = bf16[496,4096]{1,0:T(8,128)(2,1)} reshape(bf16[8,62,64,64]{3,2,1,0:T(8,128)(2,1)} %copy.23) | data formatting | bytes 8126464 | tf_op jit(solution)/shard_map/reshape | solution.py:54
  352.7 11.3 %gather_fusion = bf16[512,4096]{1,0:T(8,128)(2,1)} fusion(bf16[496,4096]{1,0:T(8,128)(2,1)} %reshape.94, s32[1024]{0:T(1024)S(1)} %pad_clamp_fusion.1), kind=kCustom, calls=%fused_computation | custom fusion | bytes 8390656 | tf_op jit(solution)/shard_map/jit(_take)/gather | solution.py:56
  363.9 4.5 broadcast_select_fusion
  368.5 8.2 %all-to-all-start.2 = ((bf16[32,16,4096]{2,1,0:T(8,128)(2,1)}), bf16[32,16,4096]{2,1,0:T(8,128)(2,1)}, u32[]{:S(2)}, u32[]{:S(2)}) async-start(bf16[32,16,4096]{2,1,0:T(8,128)(2,1)} %broadcast_select_fusion), calls=%async_computation.2 | async-start | bytes 8388608 | tf_op jit(solution)/shard_map/all_to_all | solution.py:57
  376.6 52.1 %all-to-all-done.2 = bf16[32,16,4096]{2,1,0:T(8,128)(2,1)} async-done(((bf16[32,16,4096]{2,1,0:T(8,128)(2,1)}), bf16[32,16,4096]{2,1,0:T(8,128)(2,1)}, u32[]{:S(2)}, u32[]{:S(2)}) %all-to-all-start.2) | async-done | bytes 4194336 | tf_op jit(solution)/shard_map/all_to_all | solution.py:57
  428.8 11.3 %gather_fusion.1 = bf16[512,4096]{1,0:T(8,128)(2,1)} fusion(bf16[512,4096]{1,0:T(8,128)(2,1)} %bitcast.11, s32[1024]{0:T(1024)S(1)} %pad_clamp_fusion), kind=kCustom, calls=%fused_computation.1 | custom fusion | bytes 8390656 | tf_op jit(solution)/shard_map/jit(_take)/gather | solution.py:58
  440.1 6.5 %copy.24 = bf16[512,4096]{0,1:T(8,128)(2,1)} copy(bf16[512,4096]{1,0:T(8,128)(2,1)} %gather_fusion.1) | data formatting | bytes 8388608 | tf_op jit(solution)/shard_map/jit(_take)/gather | solution.py:58
  446.5 4.5 broadcast_select_fusion.1
  (9 shorter events, 0.1 us)
Async XLA Ops:
  6.5 0.7 copy-start
  6.5 0.7 copy-start.1
  6.5 281.9 %all-gather.2.cloned.1.call-start = ((), (), s32[]{:S(2)}) async-start(), calls=%async_computation.3 | async-start | bytes 39362560 | tf_op jit(solution)/shard_map/all_gather | solution.py:47
  12.0 27.3 %all-to-all-start = ((s32[32,16,1]{1,2,0:T(1,128)}), s32[32,16,1]{1,2,0:T(1,128)S(1)}, u32[]{:S(2)}, u32[]{:S(2)}) async-start(s32[32,16,1]{1,2,0:T(1,128)} %bitcast.2), calls=%async_computation | async-start | bytes 32768 | tf_op jit(solution)/shard_map/all_to_all | solution.py:35
  39.3 59.6 %all-to-all-start.1 = ((bf16[32,16,4096]{2,1,0:T(8,128)(2,1)}), bf16[32,16,4096]{2,1,0:T(8,128)(2,1)}, u32[]{:S(2)}, u32[]{:S(2)}) async-start(bf16[32,16,4096]{2,1,0:T(8,128)(2,1)} %bitcast.41), calls=%async_computation.1 | async-start | bytes 8388608 | tf_op jit(solution)/shard_map/all_to_all | solution.py:34
  368.5 60.3 %all-to-all-start.2 = ((bf16[32,16,4096]{2,1,0:T(8,128)(2,1)}), bf16[32,16,4096]{2,1,0:T(8,128)(2,1)}, u32[]{:S(2)}, u32[]{:S(2)}) async-start(bf16[32,16,4096]{2,1,0:T(8,128)(2,1)} %broadcast_select_fusion), calls=%async_computation.2 | async-start | bytes 8388608 | tf_op jit(solution)/shard_map/all_to_all | solution.py:57
Sparse Core Ops, SparseCore 0:
  9.0 279.3 all-gather.1
where the time goes:
time: 460 us; the launch traced here: 458 us
  waiting for transfers between devices  247 us (54%)
  local copies, waits for them, and re-layouts  138 us (30%)
  starting transfers between devices  25.1 us (5%)
  matrix products  23.6 us (5%)
  between operations  13.5 us (3%)
  other arithmetic  11.1 us (2%)
    all_gather x1, waiting for transfers between devices, body(): lax.all_gather(cycle_panel, 'grp', axis=0, tiled=True)  143 us
    all_to_all x1, waiting for transfers between devices, body(): lax.all_to_all(answer, 'tile', split_axis=0, concat_axis=0, tiled=True)  52.1 us
    all_to_all x1, waiting for transfers between devices, body(): lax.all_to_all(send_tiles, 'tile', split_axis=0, concat_axis=0, tiled=True)  50.8 us
    dot_general x1, matrix products, body(): jnp.dot(dense, lax.all_gather(cycle_panel, 'grp', axis=0, tiled=True), pr...  23.6 us
    gather x2, local copies, waits for them, and re-layouts, body(): result = jnp.take(returned, position, axis=0, mode='fill', fill_value=0)  17.8 us
    transpose x1, local copies, waits for them, and re-layouts, body(): dense = dense.reshape(ROWT_DEV, nvt, edge, edge).transpose(0, 2, 1, 3).re...  12.2 us
    reshape x1, local copies, waits for them, and re-layouts, body(): dense.reshape(ROWT_DEV, nvt, edge, edge).transpose(0, 2, 1, 3)  12.1 us
    transpose x1, local copies, waits for them, and re-layouts, body(): blocks_out = cycle.reshape(ROWT_DEV, edge, nvt, edge).transpose(0, 2, 1,...  11.7 us
  transfers between devices with their start and end apart: 4, of which 3 were waited for; matrix products, arithmetic and copies ran while one was open for 15% of the time, Pallas kernels for 0%

commit v1 on v0

--- a/solution.py
+++ b/solution.py
@@ -4,6 +4,19 @@
 from jax.sharding import PartitionSpec as P
 
 ROWT_DEV = 8
+
+
+def collect(x, axis, dim):
+    ways = lax.axis_size(axis)
+    up = [(d, (d + 1) % ways) for d in range(ways)]
+    down = [(d, (d - 1) % ways) for d in range(ways)]
+    earlier, later = ([x], [x])
+    for _ in range(ways // 2):
+        earlier.append(lax.ppermute(earlier[-1], axis, up))
+    for _ in range((ways - 1) // 2):
+        later.append(lax.ppermute(later[-1], axis, down))
+    line = jnp.concatenate([*earlier[::-1], *later[1:]], axis=dim)
+    return jnp.roll(line, (lax.axis_index(axis) - ways // 2) * x.shape[dim], axis=dim)
 
 
 def body(amp_tiles, amp_row, amp_col, cycle_panel):
@@ -42,11 +55,7 @@
         .transpose(0, 2, 1, 3)
         .reshape(ROWT_DEV * edge, width)
     )
-    cycle = jnp.dot(
-        dense,
-        lax.all_gather(cycle_panel, "grp", axis=0, tiled=True),
-        preferred_element_type=jnp.float32,
-    )
+    cycle = jnp.dot(dense, collect(cycle_panel, "grp", 0), preferred_element_type=jnp.float32)
     cycle = cycle.astype(jnp.bfloat16)
     blocks_out = (
         cycle.reshape(ROWT_DEV, edge, nvt, edge)

time: 460 us -> 568 us (1.23); the launches traced: 458 us -> 557 us
  waiting for transfers between devices: 247 us -> 303 us
  local copies, waits for them, and re-layouts: 138 us -> 186 us
  between operations: 13.5 us -> 0.35 us
  starting transfers between devices: 25.1 us -> 32.8 us
    ppermute x0 -> x3, waiting for transfers between devices: none -> 201 us  [the longest x2 201 us: collect(): earlier.append(lax.ppermute(earlier[-1], axis, up))]
    all_gather x1 -> x0, waiting for transfers between devices: 143 us -> none  [body(): lax.all_gather(cycle_panel, 'grp', axis=0, tiled=True)]
    unnamed x4 -> x13, local copies, waits for them, and re-layouts: 0.01 us -> 42.2 us
    concatenate x0 -> x1, local copies, waits for them, and re-layouts: none -> 6.99 us  [collect(): jnp.roll(line, (lax.axis_index(axis) - ways // 2) * x.shape[dim], axis=dim)]
  transfers between devices with their start and end apart: 4 -> 6, of which waited for: 3 -> 4; matrix products, arithmetic and copies ran while one was open for 15% -> 16% of each run, Pallas kernels for 0% -> 0%
where the time goes in v1:
time: 568 us; the launch traced here: 557 us
  waiting for transfers between devices  303 us (53%)
  local copies, waits for them, and re-layouts  186 us (33%)
  starting transfers between devices  32.8 us (6%)
  matrix products  22.9 us (4%)
  other arithmetic  12.5 us (2%)
    ppermute x2, waiting for transfers between devices, collect(): earlier.append(lax.ppermute(earlier[-1], axis, up))  201 us
    all_to_all x1, waiting for transfers between devices, body(): lax.all_to_all(answer, 'tile', split_axis=0, concat_axis=0, tiled=True)  52.1 us
    all_to_all x1, waiting for transfers between devices, body(): lax.all_to_all(send_tiles, 'tile', split_axis=0, concat_axis=0, tiled=True)  50.6 us
    unnamed x13, local copies, waits for them, and re-layouts  42.2 us
    dot_general x1, matrix products, body(): jnp.dot(dense, collect(cycle_panel, 'grp', 0), preferred_element_type=jnp...  22.9 us
    gather x2, local copies, waits for them, and re-layouts, body(): result = jnp.take(returned, position, axis=0, mode='fill', fill_value=0)  17.8 us
    reshape x1, local copies, waits for them, and re-layouts, body(): dense.reshape(ROWT_DEV, nvt, edge, edge).transpose(0, 2, 1, 3)  12.1 us
    transpose x1, local copies, waits for them, and re-layouts, body(): dense = dense.reshape(ROWT_DEV, nvt, edge, edge).transpose(0, 2, 1, 3).re...  12.1 us
  transfers between devices with their start and end apart: 6, of which 4 were waited for; matrix products, arithmetic and copies ran while one was open for 16% of the time, Pallas kernels for 0%

profile of v1, /device:TPU:1, one launch (start us, length us, event | category | flops | bytes accessed | tf_op | source)
XLA Modules:
  0.0 557.5 jit_solution(18403568870167409698)
XLA Ops:
  0.0 2.1 collective-permute-start
  2.1 170.7 %collective-permute-done = bf16[992,3968]{1,0:T(8,128)(2,1)} collective-permute-done((bf16[992,3968]{1,0:T(8,128)(2,1)}, bf16[992,3968]{1,0:T(8,128)(2,1)}, u32[]{:S(2)}, u32[]{:S(2)}) %collective-permute-start) | collective-permute-done | bytes 7872544 | tf_op jit(solution)/shard_map/ppermute | solution.py:15
  172.9 0.0 collective-permute-start.1
  172.9 2.7 collective-permute-start.2
  175.5 0.7 fusion.14
  176.3 1.2 reduce-window.6
  177.4 0.2 slice_reduce_fusion
  177.7 0.1 fusion.10
  177.8 0.7 compare_and_fusion.1
  178.5 2.4 scatter_custom_fusion
  180.9 0.7 all_to_all.24
  181.6 9.8 %all-to-all-start = ((s32[32,16,1]{1,2,0:T(1,128)}), s32[32,16,1]{1,2,0:T(1,128)S(1)}, u32[]{:S(2)}, u32[]{:S(2)}) async-start(s32[32,16,1]{1,2,0:T(1,128)} %bitcast.2), calls=%async_computation | async-start | bytes 32768 | tf_op jit(solution)/shard_map/all_to_all | solution.py:48
  191.5 6.3 %copy.20 = bf16[512,4096]{1,0:T(8,128)(2,1)} copy(bf16[512,4096]{0,1:T(8,128)(2,1)} %bitcast.47) | data formatting | bytes 8388608 | tf_op jit(solution)/shard_map/reshape | solution.py:39
  197.8 10.2 %scatter_custom_fusion.1 = bf16[512,4096]{1,0:T(8,128)(2,1)} fusion(s32[512]{0:T(512)S(1)} %get-tuple-element.6, bf16[512,4096]{1,0:T(8,128)(2,1)} %copy.20, bf16[]{:T(256)} %constant.103.clone.1), kind=kCustom, calls=%fused_computation.10 | custom fusion | bytes 4194816 | tf_op jit(solution)/shard_map/scatter | solution.py:41
  208.0 0.0 all-to-all-done
  208.0 8.1 %all-to-all-start.1 = ((bf16[32,16,4096]{2,1,0:T(8,128)(2,1)}), bf16[32,16,4096]{2,1,0:T(8,128)(2,1)}, u32[]{:S(2)}, u32[]{:S(2)}) async-start(bf16[32,16,4096]{2,1,0:T(8,128)(2,1)} %bitcast.45), calls=%async_computation.1 | async-start | bytes 8388608 | tf_op jit(solution)/shard_map/all_to_all | solution.py:47
  216.1 0.5 broadcast.122
  216.6 0.7 reduce.5
  217.3 0.1 all_to_all.27
  217.4 50.6 %all-to-all-done.1 = bf16[32,16,4096]{2,1,0:T(8,128)(2,1)} async-done(((bf16[32,16,4096]{2,1,0:T(8,128)(2,1)}), bf16[32,16,4096]{2,1,0:T(8,128)(2,1)}, u32[]{:S(2)}, u32[]{:S(2)}) %all-to-all-start.1) | async-done | bytes 4194336 | tf_op jit(solution)/shard_map/all_to_all | solution.py:47
  268.0 10.4 %scatter_custom_fusion.2 = bf16[496,4096]{1,0:T(8,128)(2,1)} fusion(s32[512]{0:T(512)S(1)} %bitcast.51, bf16[512,4096]{1,0:T(8,128)(2,1)} %bitcast.7, bf16[]{:T(256)} %constant.103.clone.1), kind=kCustom, calls=%fused_computation.12 | custom fusion | bytes 4063744 | tf_op jit(solution)/shard_map/scatter | solution.py:51
  278.4 12.1 %reshape.91 = bf16[8,62,64,64]{3,2,1,0:T(8,128)(2,1)} reshape(bf16[496,4096]{1,0:T(8,128)(2,1)} %scatter_custom_fusion.2) | data formatting | bytes 8126464 | tf_op jit(solution)/shard_map/reshape | solution.py:54
  290.5 12.1 %copy.21 = bf16[8,64,62,64]{1,0,3,2:T(8,128)(2,1)} copy(bf16[8,64,62,64]{3,1,2,0:T(8,128)(2,1)} %bitcast.40) | data formatting | bytes 8126464 | tf_op jit(solution)/shard_map/transpose | solution.py:55
  302.5 11.5 %reshape.92 = bf16[512,3968]{0,1:T(8,128)(2,1)} reshape(bf16[8,64,62,64]{1,0,3,2:T(8,128)(2,1)} %copy.21) | data formatting | bytes 8126464 | tf_op jit(solution)/shard_map/reshape | solution.py:56
  314.0 29.9 %collective-permute-done.1 = bf16[992,3968]{1,0:T(8,128)(2,1)} collective-permute-done((bf16[992,3968]{1,0:T(8,128)(2,1)}, bf16[992,3968]{1,0:T(8,128)(2,1)}, u32[]{:S(2)}, u32[]{:S(2)}) %collective-permute-start.1) | collective-permute-done | bytes 7872544 | tf_op jit(solution)/shard_map/ppermute | solution.py:15
  344.0 0.0 slice-start
  344.0 7.0 %constant_dynamic-update-slice_fusion.7 = bf16[7936,3968]{1,0:T(8,128)(2,1)} fusion(bf16[992,3968]{1,0:T(8,128)(2,1)} %collective-permute-done.1), kind=kLoop, calls=%fused_computation.30 | loop fusion | bytes 15745024
  351.0 0.0 slice-start.1
  351.0 7.1 %constant_dynamic-update-slice_fusion.6 = bf16[7936,3968]{1,0:T(8,128)(2,1)} fusion(bf16[7936,3968]{1,0:T(8,128)(2,1)} %constant_dynamic-update-slice_fusion.7, bf16[992,3968]{1,0:T(8,128)(2,1)} %collective-permute-done), kind=kLoop, calls=%fused_computation.29 | loop fusion | bytes 15745024
  358.1 0.0 slice-done
  358.1 0.0 slice-done.1
  358.1 3.6 constant_dynamic-update-slice_fusion.5
  361.7 0.0 collective-permute-done.2
  361.7 6.9 %constant_dynamic-update-slice_fusion.4 = bf16[7936,3968]{1,0:T(8,128)(2,1)} fusion(bf16[7936,3968]{1,0:T(8,128)(2,1)} %constant_dynamic-update-slice_fusion.5, bf16[992,3968]{1,0:T(8,128)(2,1)} %collective-permute-done.2), kind=kLoop, calls=%fused_computation.27 | loop fusion | bytes 15745024
  368.6 7.0 %constant_dynamic-update-slice_fusion.3 = bf16[7936,3968]{1,0:T(8,128)(2,1)} fusion(bf16[7936,3968]{1,0:T(8,128)(2,1)} %constant_dynamic-update-slice_fusion.4, bf16[992,3968]{1,0:T(8,128)(2,1)} %collective-permute-done.1), kind=kLoop, calls=%fused_computation.26 | loop fusion | bytes 15745024
  375.6 6.9 %constant_dynamic-update-slice_fusion.2 = bf16[7936,3968]{1,0:T(8,128)(2,1)} fusion(bf16[7936,3968]{1,0:T(8,128)(2,1)} %constant_dynamic-update-slice_fusion.3, bf16[992,3968]{1,0:T(8,128)(2,1)} %collective-permute-done), kind=kLoop, calls=%fused_computation.25 | loop fusion | bytes 15745024
  382.5 3.7 constant_dynamic-update-slice_fusion.1
  386.2 0.0 copy-start
  386.2 7.0 %constant_dynamic-update-slice_fusion = bf16[7936,3968]{1,0:T(8,128)(2,1)} fusion(bf16[7936,3968]{1,0:T(8,128)(2,1)} %constant_dynamic-update-slice_fusion.1, bf16[992,3968]{1,0:T(8,128)(2,1)} %collective-permute-done.2), kind=kLoop, calls=%fused_computation.23 | loop fusion | bytes 15745024 | tf_op jit(solution)/shard_map/jit(_roll_dynamic)/concatenate | solution.py:19
  393.2 0.0 copy-done
  393.2 22.9 %fusion.2 = bf16[512,3968]{1,0:T(8,128)(2,1)} fusion(bf16[512,3968]{0,1:T(8,128)(2,1)S(1)} %copy-done, bf16[7936,3968]{1,0:T(8,128)(2,1)} %constant_dynamic-update-slice_fusion, s32[]{:T(128)S(6)} %select_n.72), kind=kOutput, calls=%fused_computation.7 | convolution fusion | flops 16124936192 | bytes 39616516 | tf_op jit(solution)/shard_map/dot_general | solution.py:58
  416.1 6.5 %copy.22 = bf16[512,3968]{0,1:T(8,128)(2,1)} copy(bf16[512,3968]{1,0:T(8,128)(2,1)} %fusion.2) | data formatting | bytes 8126464 | tf_op jit(solution)/shard_map/convert_element_type | solution.py:59
  422.5 10.9 %reshape.93 = bf16[8,64,62,64]{1,0,3,2:T(8,128)(2,1)} reshape(bf16[512,3968]{0,1:T(8,128)(2,1)} %copy.22) | data formatting | bytes 8126464 | tf_op jit(solution)/shard_map/reshape | solution.py:61
  433.4 11.9 %copy.23 = bf16[8,62,64,64]{3,2,1,0:T(8,128)(2,1)} copy(bf16[8,62,64,64]{2,0,3,1:T(8,128)(2,1)} %bitcast.41) | data formatting | bytes 8126464 | tf_op jit(solution)/shard_map/transpose | solution.py:62
  445.3 11.7 %reshape.94 = bf16[496,4096]{1,0:T(8,128)(2,1)} reshape(bf16[8,62,64,64]{3,2,1,0:T(8,128)(2,1)} %copy.23) | data formatting | bytes 8126464 | tf_op jit(solution)/shard_map/reshape | solution.py:63
  457.0 11.3 %gather_fusion = bf16[512,4096]{1,0:T(8,128)(2,1)} fusion(bf16[496,4096]{1,0:T(8,128)(2,1)} %reshape.94, s32[1024]{0:T(1024)S(1)} %pad_clamp_fusion.1), kind=kCustom, calls=%fused_computation | custom fusion | bytes 8390656 | tf_op jit(solution)/shard_map/jit(_take)/gather | solution.py:65
  468.2 4.5 broadcast_select_fusion
  472.8 10.1 %all-to-all-start.2 = ((bf16[32,16,4096]{2,1,0:T(8,128)(2,1)}), bf16[32,16,4096]{2,1,0:T(8,128)(2,1)}, u32[]{:S(2)}, u32[]{:S(2)}) async-start(bf16[32,16,4096]{2,1,0:T(8,128)(2,1)} %broadcast_select_fusion), calls=%async_computation.2 | async-start | bytes 8388608 | tf_op jit(solution)/shard_map/all_to_all | solution.py:66
  482.9 52.1 %all-to-all-done.2 = bf16[32,16,4096]{2,1,0:T(8,128)(2,1)} async-done(((bf16[32,16,4096]{2,1,0:T(8,128)(2,1)}), bf16[32,16,4096]{2,1,0:T(8,128)(2,1)}, u32[]{:S(2)}, u32[]{:S(2)}) %all-to-all-start.2) | async-done | bytes 4194336 | tf_op jit(solution)/shard_map/all_to_all | solution.py:66
  535.0 11.3 %gather_fusion.1 = bf16[512,4096]{1,0:T(8,128)(2,1)} fusion(bf16[512,4096]{1,0:T(8,128)(2,1)} %bitcast.11, s32[1024]{0:T(1024)S(1)} %pad_clamp_fusion), kind=kCustom, calls=%fused_computation.1 | custom fusion | bytes 8390656 | tf_op jit(solution)/shard_map/jit(_take)/gather | solution.py:67
  546.3 6.5 %copy.24 = bf16[512,4096]{0,1:T(8,128)(2,1)} copy(bf16[512,4096]{1,0:T(8,128)(2,1)} %gather_fusion.1) | data formatting | bytes 8388608 | tf_op jit(solution)/shard_map/jit(_take)/gather | solution.py:67
  552.8 4.5 broadcast_select_fusion.1
  (8 shorter events, 0.1 us)
Async XLA Ops:
  0.0 172.9 %collective-permute-start = (bf16[992,3968]{1,0:T(8,128)(2,1)}, bf16[992,3968]{1,0:T(8,128)(2,1)}, u32[]{:S(2)}, u32[]{:S(2)}) collective-permute-start(bf16[992,3968]{1,0:T(8,128)(2,1)} %param.7), channel_id=1, source_target_pairs={{0,32},{32,64},{64,96},{96,0},{1,33},{33,65},{65,97},{97,1},{2,34}... | collective-permute-start | bytes 23617544 | tf_op jit(solution)/shard_map/ppermute | solution.py:15
  172.9 171.1 %collective-permute-start.1 = (bf16[992,3968]{1,0:T(8,128)(2,1)}, bf16[992,3968]{1,0:T(8,128)(2,1)}, u32[]{:S(2)}, u32[]{:S(2)}) collective-permute-start(bf16[992,3968]{1,0:T(8,128)(2,1)} %collective-permute-done), channel_id=1, source_target_pairs={{0,32},{32,64},{64,96},{96,0},{1,33},{33,65},{65,97},{97,1},{2,34}... | collective-permute-start | bytes 23617544 | tf_op jit(solution)/shard_map/ppermute | solution.py:15
  172.9 188.8 %collective-permute-start.2 = (bf16[992,3968]{1,0:T(8,128)(2,1)}, bf16[992,3968]{1,0:T(8,128)(2,1)}, u32[]{:S(2)}, u32[]{:S(2)}) collective-permute-start(bf16[992,3968]{1,0:T(8,128)(2,1)} %param.7), channel_id=1, source_target_pairs={{0,96},{32,0},{64,32},{96,64},{1,97},{33,1},{65,33},{97,65},{2,98}... | collective-permute-start | bytes 23617544 | tf_op jit(solution)/shard_map/ppermute | solution.py:17
  181.6 26.4 %all-to-all-start = ((s32[32,16,1]{1,2,0:T(1,128)}), s32[32,16,1]{1,2,0:T(1,128)S(1)}, u32[]{:S(2)}, u32[]{:S(2)}) async-start(s32[32,16,1]{1,2,0:T(1,128)} %bitcast.2), calls=%async_computation | async-start | bytes 32768 | tf_op jit(solution)/shard_map/all_to_all | solution.py:48
  208.0 60.0 %all-to-all-start.1 = ((bf16[32,16,4096]{2,1,0:T(8,128)(2,1)}), bf16[32,16,4096]{2,1,0:T(8,128)(2,1)}, u32[]{:S(2)}, u32[]{:S(2)}) async-start(bf16[32,16,4096]{2,1,0:T(8,128)(2,1)} %bitcast.45), calls=%async_computation.1 | async-start | bytes 8388608 | tf_op jit(solution)/shard_map/all_to_all | solution.py:47
  344.0 14.1 %slice-start = ((s8[7872512]{0:T(1024)(128)(4,1)}), s8[4194304]{0:T(1024)(128)(4,1)S(1)}, s32[]{:S(2)}) async-start(s8[7872512]{0:T(1024)(128)(4,1)} %bitcast.42), calls=%async_computation.3 | async-start | bytes 8388608
  351.0 7.1 %slice-start.1 = ((s8[7872512]{0:T(1024)(128)(4,1)}), s8[3678208]{0:T(1024)(128)(4,1)S(1)}, s32[]{:S(2)}) async-start(s8[7872512]{0:T(1024)(128)(4,1)} %bitcast.42), calls=%async_computation.4 | async-start | bytes 7356416
  386.2 7.0 %copy-start = (bf16[512,3968]{0,1:T(8,128)(2,1)S(1)}, bf16[512,3968]{0,1:T(8,128)(2,1)}, u32[]{:S(2)}) copy-start(bf16[512,3968]{0,1:T(8,128)(2,1)} %reshape.92) | copy-start | bytes 12189700
  472.8 62.2 %all-to-all-start.2 = ((bf16[32,16,4096]{2,1,0:T(8,128)(2,1)}), bf16[32,16,4096]{2,1,0:T(8,128)(2,1)}, u32[]{:S(2)}, u32[]{:S(2)}) async-start(bf16[32,16,4096]{2,1,0:T(8,128)(2,1)} %broadcast_select_fusion), calls=%async_computation.2 | async-start | bytes 8388608 | tf_op jit(solution)/shard_map/all_to_all | solution.py:66
